TPU v7x, 32 devices: a whole 2x2x4 slice. The times are simulated.
32 devices in a mesh: pulse: 16 (over z, x, core), range: 2 (over y).
Axes of the slice: x: 2, y: 2, z: 4, core: 2. Of those that a mesh axis runs over, the one named last changes fastest.
Arguments:
- echo: bfloat16 [32, 2, 32768], P('pulse', None, 'range'), may hold values from -6 to 6
- chirp_phase: float32 [256], replicated, may hold values from -0.5 to 201.5624
- rec_phase: float32 [2, 2048, 2], P('range', 'pulse'), may hold values from -3.140625 to 3.140625
- rec_start: int32 [2, 2048], P('range', 'pulse'), may hold values from 0 to 32256
- rec_owner: int32 [2, 2048, 1], P('range', 'pulse'), may hold values from 0 to 31; in each aligned block of 128 rows (0 to 127, 128 to 255, ..., all dimensions but the last counted through in order) at most 6 rows name the same one
- rec_row: int32 [2, 2048], P('range', 'pulse'), may hold values from 0 to 63
- rec_weight: float32 [2, 2048], P('range', 'pulse'), may hold values from 0.2 to 1
- rec_count: int32 [2, 16], P('range', 'pulse'), may hold values from 96 to 128, as said below
- prior: bfloat16 [512, 2, 1024], P('pulse', None, 'range'), may hold values from -6 to 6
- interp_weight: bfloat16 [64, 32], replicated, may hold values from -1 to 1
Outputs:
- tiles: float32 [1024, 2, 1024], P('pulse', None, 'range')
Inputs may be any that keep to these rules, and one draw needn't show every extreme that they name: `rec_owner`: in each aligned block of 128 record slots (one device's slots) no owner is named more than 6 times. Owner o is the tile of pulse index o // 2 and range index o % 2, 2 being the number of range devices. `rec_count`: some subimage has all 128 slots live.
All inputs are finite; a program needn't handle non-finite values.
Results may differ from a plain program's by a relative error of at most 0.0034.
Values may be sent and summed in bfloat16 or wider, within the bound.
No kernel may reach another device: no remote copies, remote signals or barrier semaphores. Data moves between devices by JAX's collectives and lax.ppermute only.
A program may use at most 64 MiB of HBM per device.

v0:
```python
import jax
import jax.numpy as jnp
from jax import lax
from jax.sharding import PartitionSpec as P

SEG = 512


def chirp_matrix(chirp_phase):
    tap_count = chirp_phase.shape[0]
    tap_scale = 1.0 / jnp.sqrt(jnp.float32(tap_count))
    real_taps = jnp.cos(chirp_phase) * tap_scale
    imag_taps = jnp.sin(chirp_phase) * tap_scale

    def banded(values):
        padded = jnp.concatenate([values, jnp.zeros((tap_count + 1,), jnp.float32)])
        return (
            jnp.tile(padded, tap_count)[: 2 * tap_count * tap_count]
            .reshape(tap_count, 2 * tap_count)
            .T
        )

    real_band = banded(real_taps)
    imag_band = banded(imag_taps)
    upper = jnp.concatenate([real_band, -imag_band], axis=1)
    lower = jnp.concatenate([imag_band, real_band], axis=1)
    return jnp.concatenate([upper, lower], axis=0).astype(jnp.bfloat16)


def compress(echo_block, tail_rim, filter_matrix):
    pulses, planes, bin_count = echo_block.shape
    tap_count = filter_matrix.shape[1] // 2
    block_count = bin_count // tap_count
    extended = jnp.concatenate([echo_block, tail_rim], axis=2)
    left_half = extended[:, :, :bin_count].reshape(pulses, planes, block_count, tap_count)
    right_half = extended[:, :, tap_count:].reshape(pulses, planes, block_count, tap_count)
    windows = jnp.concatenate([left_half, right_half], axis=3)
    windows = windows.transpose(0, 2, 1, 3).reshape(pulses * block_count, 2 * planes * tap_count)
    filtered = jnp.dot(windows, filter_matrix, preferred_element_type=jnp.float32)
    filtered = filtered.reshape(pulses, block_count, planes, tap_count).transpose(0, 2, 1, 3)
    return filtered.reshape(pulses, planes, bin_count).astype(jnp.bfloat16)


def cut_windows(block_table, starts):
    block_total = block_table.shape[0]
    first_block = starts // SEG
    second_block = jnp.minimum(first_block + 1, block_total - 1)
    offsets = starts % SEG
    paired = jnp.concatenate([block_table[first_block], block_table[second_block]], axis=3)
    for bit_number in range((SEG - 1).bit_length()):
        step_size = 1 << bit_number
        moved = jnp.concatenate(
            [paired[..., step_size:], jnp.zeros(paired.shape[:-1] + (step_size,), paired.dtype)],
            axis=3,
        )
        chosen = (offsets // step_size % 2 == 1)[:, None, None, None]
        paired = jnp.where(chosen, moved, paired)
    return paired[..., :SEG]


def form_records(block_table, starts, phases, scales):
    windows = cut_windows(block_table, starts)
    cosine = jnp.cos(phases).astype(jnp.bfloat16)
    sine_part = jnp.sin(phases).astype(jnp.bfloat16)
    real_part = windows[:, :, 0]
    imag_part = windows[:, :, 1]
    out_real = jnp.einsum(
        "bk,bks->bs", cosine, real_part, preferred_element_type=jnp.float32
    ) - jnp.einsum("bk,bks->bs", sine_part, imag_part, preferred_element_type=jnp.float32)
    out_imag = jnp.einsum(
        "bk,bks->bs", cosine, imag_part, preferred_element_type=jnp.float32
    ) + jnp.einsum("bk,bks->bs", sine_part, real_part, preferred_element_type=jnp.float32)
    return (jnp.stack([out_real, out_imag], axis=1) * scales[:, None, None]).astype(jnp.bfloat16)


def on_device(
    echo,
    chirp_phase,
    rec_phase,
    rec_start,
    rec_owner,
    rec_row,
    rec_weight,
    rec_count,
    prior,
    interp_weight,
):
    filter_matrix = chirp_matrix(chirp_phase)
    tap_count = chirp_phase.shape[0]
    raw_echo = lax.all_gather(echo, "range", axis=2, tiled=True)
    profiles = compress(raw_echo, jnp.zeros_like(raw_echo[:, :, :tap_count]), filter_matrix)
    pulses, planes, bin_total = profiles.shape
    block_table = profiles.reshape(pulses, planes, bin_total // SEG, SEG).transpose(2, 0, 1, 3)
    slot_count = rec_start.shape[1]
    starts = rec_start[0]
    phases = rec_phase[0]
    owners = rec_owner[0, :, 0]
    dest_rows = rec_row[0]
    weights = rec_weight[0]
    live_mask = (jnp.arange(slot_count) < rec_count[0, 0]).astype(jnp.float32)
    scales = live_mask * weights / jnp.sqrt(jnp.float32(pulses))
    block_size = min(64, slot_count)
    group_count = slot_count // block_size

    def form_group(items):
        return form_records(block_table, items[0], items[1], items[2])

    records = lax.map(
        form_group,
        (
            starts.reshape(group_count, block_size),
            phases.reshape(group_count, block_size, pulses),
            scales.reshape(group_count, block_size),
        ),
    )
    records = records.reshape(slot_count, 2 * SEG)
    pulse_count = lax.axis_size("pulse")
    range_count = lax.axis_size("range")
    owner_total = pulse_count * range_count
    capacity = max(2, 3 * slot_count // (2 * owner_total))
    owner_marks = (owners[:, None] == jnp.arange(owner_total)[None, :]).astype(jnp.int32)
    earlier = jnp.cumsum(owner_marks, axis=0) - owner_marks
    slot_rank = jnp.sum(earlier * owner_marks, axis=1)
    slot_index = owners * capacity + slot_rank
    placement = slot_index[None, :] == jnp.arange(owner_total * capacity)[:, None]
    outgoing = jnp.dot(
        placement.astype(jnp.bfloat16), records, preferred_element_type=jnp.float32
    ).astype(jnp.bfloat16)
    row_slots = jnp.sum(placement.astype(jnp.int32) * dest_rows[None, :], axis=1)
    outgoing = outgoing.reshape(pulse_count, range_count, capacity, 2, SEG)
    row_slots = row_slots.reshape(pulse_count, range_count, capacity)
    incoming, incoming_rows = (
        lax.all_to_all(
            lax.all_to_all(outgoing, "pulse", split_axis=0, concat_axis=0, tiled=True),
            "range",
            split_axis=1,
            concat_axis=1,
            tiled=True,
        ),
        lax.all_to_all(
            lax.all_to_all(row_slots, "pulse", split_axis=0, concat_axis=0, tiled=True),
            "range",
            split_axis=1,
            concat_axis=1,
            tiled=True,
        ),
    )
    incoming = incoming.reshape(-1, 2, SEG)
    incoming_rows = incoming_rows.reshape(-1)
    out_rows = interp_weight.shape[0]
    tile_image = jnp.einsum("rm,mcs->rcs", interp_weight, prior, preferred_element_type=jnp.float32)
    row_table = (incoming_rows[:, None] == jnp.arange(out_rows)[None, :]).astype(jnp.bfloat16)
    tile_image = tile_image + jnp.einsum(
        "jr,jcs->rcs", row_table, incoming, preferred_element_type=jnp.float32
    )
    return tile_image


def solution(mesh):
    placed = (
        P("pulse", None, "range"),
        P(),
        P("range", "pulse", None),
        P("range", "pulse"),
        P("range", "pulse", None),
        P("range", "pulse"),
        P("range", "pulse"),
        P("range", "pulse"),
        P("pulse", None, "range"),
        P(),
    )
    return jax.shard_map(
        on_device, mesh=mesh, in_specs=placed, out_specs=P("pulse", None, "range"), check_vma=False
    )
```

profile of v0, /device:TPU:0, one launch (start us, length us, event | category | flops | bytes accessed | tf_op | source)
XLA Modules:
  0.0 105.9 jit_solution(2789000673935303853)
XLA Ops:
  4.0 7.4 %all-to-all-start = ((s32[16,2,6]{2,1,0:T(2,128)}), s32[16,2,6]{2,1,0:T(2,128)S(1)}, u32[]{:S(2)}, u32[]{:S(2)}) async-start(s32[16,2,6]{2,1,0:T(2,128)} %reshape.452), calls=%async_computation | async-start | bytes 32768 | tf_op jit(solution)/shard_map/all_to_all | solution.py:141
  14.1 6.5 %all_gather.3 = bf16[2,2,32768]{2,1,0:T(2,128)(2,1)S(1)} all-gather(bf16[2,2,16384]{2,1,0:T(2,128)(2,1)S(1)} %copy-done.1), channel_id=1, replica_groups=mesh['pulse'=16,'range'=2] {'range'}, dimensions={2}, use_global_device_ids=true | all-gather | bytes 393216 | tf_op jit(solution)/shard_map/all_gather | solution.py:90
  26.1 42.6 %while.13 = (s32[]{:T(128)}, bf16[2,64,2,512]{3,2,1,0:T(2,128)(2,1)S(1)}, f32[2,64,2]{1,0,2:T(2,128)S(1)}, s32[2,64]{1,0:T(2,128)S(1)}, bf16[64,2,2,512]{3,2,1,0...) while((s32[]{:T(128)}, bf16[2,64,2,512]{3,2,1,0:T(2,128)(2,1)S(1)}, f32[2,64,2]{1,0,2:T(2,128)S(1)}, ...), condition=%wide.region_4.5_spmd, body=%wide.region_3.4_spmd.sunk | while | flops 3162434 | bytes 28723936 | solution.py:108
  26.3 1.1 %gather_fusion = bf16[64,2,2,512]{3,2,1,0:T(2,128)(2,1)S(1)} fusion(bf16[64,2,2,512]{3,2,1,0:T(2,128)(2,1)S(1)} %get-tuple-element.289, s32[1024]{0:T(1024)S(1)} %get-tuple-element.256), kind=kCustom, calls=%fused_computation.clone.1 | custom fusion | bytes 524544 | tf_op jit(solution)/shard_map/while/body/eval_jaxpr/gather | solution.py:49
  27.6 1.1 %gather_fusion.1 = bf16[64,2,2,512]{3,2,1,0:T(2,128)(2,1)S(1)} fusion(bf16[64,2,2,512]{3,2,1,0:T(2,128)(2,1)S(1)} %get-tuple-element.289, s32[1024]{0:T(1024)S(1)} %get-tuple-element.257), kind=kCustom, calls=%fused_computation.1.clone.1 | custom fusion | bytes 524544 | tf_op jit(solution)/shard_map/while/body/eval_jaxpr/gather | solution.py:49
  28.9 1.0 slice.134
  31.0 1.0 slice.135
  33.0 1.0 slice.136
  34.0 1.0 broadcast_select_fusion.20
  35.0 1.0 slice.137
  36.0 1.0 broadcast_select_fusion.21
  37.0 1.0 slice.138
  39.0 1.0 slice.139
  41.0 1.0 slice.140
  42.0 1.0 broadcast_select_fusion.24
  47.5 1.1 %gather_fusion = bf16[64,2,2,512]{3,2,1,0:T(2,128)(2,1)S(1)} fusion(bf16[64,2,2,512]{3,2,1,0:T(2,128)(2,1)S(1)} %get-tuple-element.289, s32[1024]{0:T(1024)S(1)} %get-tuple-element.256), kind=kCustom, calls=%fused_computation.clone.1 | custom fusion | bytes 524544 | tf_op jit(solution)/shard_map/while/body/eval_jaxpr/gather | solution.py:49
  48.8 1.1 %gather_fusion.1 = bf16[64,2,2,512]{3,2,1,0:T(2,128)(2,1)S(1)} fusion(bf16[64,2,2,512]{3,2,1,0:T(2,128)(2,1)S(1)} %get-tuple-element.289, s32[1024]{0:T(1024)S(1)} %get-tuple-element.257), kind=kCustom, calls=%fused_computation.1.clone.1 | custom fusion | bytes 524544 | tf_op jit(solution)/shard_map/while/body/eval_jaxpr/gather | solution.py:49
  50.2 1.0 slice.134
  52.2 1.0 slice.135
  54.2 1.0 slice.136
  56.2 1.0 slice.137
  58.2 1.0 slice.138
  60.2 1.0 slice.139
  62.2 1.0 slice.140
  69.0 1.0 reshape.458
  70.0 5.9 %all-to-all-start.2 = ((bf16[16,2,6,2,512]{4,3,2,1,0:T(2,128)(2,1)}), bf16[16,2,6,2,512]{4,3,2,1,0:T(2,128)(2,1)S(1)}, u32[]{:S(2)}, u32[]{:S(2)}) async-start(bf16[16,2,6,2,512]{4,3,2,1,0:T(2,128)(2,1)} %reshape.458), calls=%async_computation.2 | async-start | bytes 786432 | tf_op jit(solution)/shard_map/all_to_all | solution.py:134
  76.6 11.5 %all-to-all-done.2 = bf16[16,2,6,2,512]{4,3,2,1,0:T(2,128)(2,1)S(1)} async-done(((bf16[16,2,6,2,512]{4,3,2,1,0:T(2,128)(2,1)}), bf16[16,2,6,2,512]{4,3,2,1,0:T(2,128)(2,1)S(1)}, u32[]{:S(2)}, u32[]{:S(2)}) %all-to-all-start.2) | async-done | bytes 393248 | tf_op jit(solution)/shard_map/all_to_all | solution.py:134
  88.1 3.2 %all-to-all-start.1 = ((s32[16,2,6]{0,2,1:T(8,128)}), s32[16,2,6]{0,2,1:T(8,128)S(1)}, u32[]{:S(2)}, u32[]{:S(2)}) async-start(s32[16,2,6]{0,2,1:T(8,128)} %copy.62), calls=%async_computation.1 | async-start | bytes 16384 | tf_op jit(solution)/shard_map/all_to_all | solution.py:140
  91.3 1.0 copy.68
  92.3 2.8 %all-to-all-done.1 = s32[16,2,6]{0,2,1:T(8,128)S(1)} async-done(((s32[16,2,6]{0,2,1:T(8,128)}), s32[16,2,6]{0,2,1:T(8,128)S(1)}, u32[]{:S(2)}, u32[]{:S(2)}) %all-to-all-start.1) | async-done | bytes 800 | tf_op jit(solution)/shard_map/all_to_all | solution.py:140
  95.1 3.5 %all-to-all-start.3 = ((bf16[16,2,6,2,512]{4,3,2,0,1:T(2,128)(2,1)}), bf16[16,2,6,2,512]{4,3,2,0,1:T(2,128)(2,1)S(1)}, u32[]{:S(2)}, u32[]{:S(2)}) async-start(bf16[16,2,6,2,512]{4,3,2,0,1:T(2,128)(2,1)} %copy.68), calls=%async_computation.3 | async-start | bytes 786432 | tf_op jit(solution)/shard_map/all_to_all | solution.py:133
  99.0 5.5 %all-to-all-done.3 = bf16[16,2,6,2,512]{4,3,2,0,1:T(2,128)(2,1)S(1)} async-done(((bf16[16,2,6,2,512]{4,3,2,0,1:T(2,128)(2,1)}), bf16[16,2,6,2,512]{4,3,2,0,1:T(2,128)(2,1)S(1)}, u32[]{:S(2)}, u32[]{:S(2)}) %all-to-all-start.3) | async-done | bytes 393248 | tf_op jit(solution)/shard_map/all_to_all | solution.py:133
  (127 shorter events, 34.7 us)
Async XLA Ops:
  0.0 98.6 %copy-start = (bf16[32,2,512]{2,1,0:T(2,128)(2,1)S(1)}, bf16[32,2,512]{2,1,0:T(2,128)(2,1)}, u32[]{:S(2)}) copy-start(bf16[32,2,512]{2,1,0:T(2,128)(2,1)} %param.20) | copy-start | bytes 196612
  4.0 66.1 %all-to-all-start = ((s32[16,2,6]{2,1,0:T(2,128)}), s32[16,2,6]{2,1,0:T(2,128)S(1)}, u32[]{:S(2)}, u32[]{:S(2)}) async-start(s32[16,2,6]{2,1,0:T(2,128)} %reshape.452), calls=%async_computation | async-start | bytes 32768 | tf_op jit(solution)/shard_map/all_to_all | solution.py:141
  12.1 0.7 copy-start.4
  13.2 0.9 copy-start.1
  21.8 1.5 %copy-start.5 = (f32[1,128]{1,0:T(1,128)S(1)}, f32[1,128]{1,0:T(1,128)}, u32[]{:S(2)}) copy-start(f32[1,128]{1,0:T(1,128)} %param.18) | copy-start | bytes 1540
  21.8 3.0 %copy-start.3 = (f32[1,128,2]{1,2,0:T(2,128)S(1)}, f32[1,128,2]{1,2,0:T(2,128)}, u32[]{:S(2)}) copy-start(f32[1,128,2]{1,2,0:T(2,128)} %param.14) | copy-start | bytes 3076
  21.8 3.6 %copy-start.6 = (s32[1,128]{1,0:T(1,128)S(1)}, s32[1,128]{1,0:T(1,128)}, u32[]{:S(2)}) copy-start(s32[1,128]{1,0:T(1,128)} %param.15) | copy-start | bytes 1540
  70.0 28.5 %copy-start.2 = (bf16[64,32]{0,1:T(8,128)(2,1)S(1)}, bf16[64,32]{0,1:T(8,128)(2,1)}, u32[]{:S(2)}) copy-start(bf16[64,32]{0,1:T(8,128)(2,1)} %param.21) | copy-start | bytes 12292
  70.0 18.0 %all-to-all-start.2 = ((bf16[16,2,6,2,512]{4,3,2,1,0:T(2,128)(2,1)}), bf16[16,2,6,2,512]{4,3,2,1,0:T(2,128)(2,1)S(1)}, u32[]{:S(2)}, u32[]{:S(2)}) async-start(bf16[16,2,6,2,512]{4,3,2,1,0:T(2,128)(2,1)} %reshape.458), calls=%async_computation.2 | async-start | bytes 786432 | tf_op jit(solution)/shard_map/all_to_all | solution.py:134
  88.1 7.0 %all-to-all-start.1 = ((s32[16,2,6]{0,2,1:T(8,128)}), s32[16,2,6]{0,2,1:T(8,128)S(1)}, u32[]{:S(2)}, u32[]{:S(2)}) async-start(s32[16,2,6]{0,2,1:T(8,128)} %copy.62), calls=%async_computation.1 | async-start | bytes 16384 | tf_op jit(solution)/shard_map/all_to_all | solution.py:140
  95.1 9.4 %all-to-all-start.3 = ((bf16[16,2,6,2,512]{4,3,2,0,1:T(2,128)(2,1)}), bf16[16,2,6,2,512]{4,3,2,0,1:T(2,128)(2,1)S(1)}, u32[]{:S(2)}, u32[]{:S(2)}) async-start(bf16[16,2,6,2,512]{4,3,2,0,1:T(2,128)(2,1)} %copy.68), calls=%async_computation.3 | async-start | bytes 786432 | tf_op jit(solution)/shard_map/all_to_all | solution.py:133
where the time goes:
time: 106 us
  local copies, waits for them, and re-layouts  31.5 us (30%)
  other arithmetic  23.3 us (22%)
  starting transfers between devices  19.9 us (19%)
  waiting for transfers between devices  19.8 us (19%)
  blocking collectives  6.46 us (6%)
  matrix products  3.38 us (3%)
    select_n x18, other arithmetic, cut_windows(): paired = jnp.where(chosen, moved, paired)  16.4 us
    slice x18, local copies, waits for them, and re-layouts, cut_windows(): paired[..., step_size:]  15.4 us
    all_to_all x1, waiting for transfers between devices, on_device(): lax.all_to_all(outgoing, 'pulse', split_axis=0, concat_axis=0, tiled=True)  11.5 us
    all_to_all x1, starting transfers between devices, on_device(): lax.all_to_all(row_slots, 'pulse', split_axis=0, concat_axis=0, tiled=True)  7.39 us
    all_gather x1, blocking collectives, on_device(): raw_echo = lax.all_gather(echo, 'range', axis=2, tiled=True)  6.46 us
    all_to_all x1, starting transfers between devices, on_device(): lax.all_to_all(outgoing, 'pulse', split_axis=0, concat_axis=0, tiled=True)  5.85 us
    all_to_all x1, waiting for transfers between devices, on_device(): lax.all_to_all(lax.all_to_all(outgoing, 'pulse', split_axis=0, concat_axi...  5.52 us
    all_to_all x1, starting transfers between devices, on_device(): lax.all_to_all(lax.all_to_all(outgoing, 'pulse', split_axis=0, concat_axi...  3.47 us
  transfers between devices with their start and end apart: 4, of which 3 were waited for; matrix products, arithmetic and copies ran while one was open for 50% of the time, Pallas kernels for 0%

commit v1 on v0

--- a/solution.py
+++ b/solution.py
@@ -87,7 +87,22 @@
 ):
     filter_matrix = chirp_matrix(chirp_phase)
     tap_count = chirp_phase.shape[0]
-    raw_echo = lax.all_gather(echo, "range", axis=2, tiled=True)
+
+    def target_replace(sample):
+        block_out, s_next = (lax.axis_size("range"), lax.axis_index("range"))
+        local_part, a_now = (sample, 1)
+        while a_now < block_out:
+            trail = []
+            for c in tuple(range(block_out)):
+                trail.append((c, c ^ a_now))
+            raw_out = lax.ppermute(local_part, "range", trail)
+            small = jnp.concatenate([local_part, raw_out], axis=2)
+            spare = jnp.concatenate([raw_out, local_part], 2)
+            local_part = jnp.where(s_next & a_now == 0, small, spare)
+            a_now = 2 * a_now
+        return local_part
+
+    raw_echo = target_replace(echo)
     profiles = compress(raw_echo, jnp.zeros_like(raw_echo[:, :, :tap_count]), filter_matrix)
     pulses, planes, bin_total = profiles.shape
     block_table = profiles.reshape(pulses, planes, bin_total // SEG, SEG).transpose(2, 0, 1, 3)

time: 106 us -> 103 us (0.972)
  blocking collectives: 6.46 us -> 0 us
  starting transfers between devices: 19.9 us -> 21.7 us
    all_gather x1 -> x0, blocking collectives: 6.46 us -> none  [on_device(): raw_echo = lax.all_gather(echo, 'range', axis=2, tiled=True)]
    ppermute x0 -> x1, starting transfers between devices: none -> 3 us  [target_replace(): raw_out = lax.ppermute(local_part, 'range', trail)]
    all_to_all x1, starting transfers between devices: 7.39 us -> 5.91 us  [on_device(): lax.all_to_all(row_slots, 'pulse', split_axis=0, concat_axis=0, tiled=True)]
  transfers between devices with their start and end apart: 4 -> 5, of which waited for: 3 -> 3; matrix products, arithmetic and copies ran while one was open for 50% -> 56% of each run, Pallas kernels for 0% -> 0%
where the time goes in v1:
time: 103 us; the launch traced here: 102 us
  local copies, waits for them, and re-layouts  31.4 us (30%)
  other arithmetic  24.3 us (24%)
  starting transfers between devices  21.7 us (21%)
  waiting for transfers between devices  19.8 us (19%)
  matrix products  3.33 us (3%)
    select_n x18, other arithmetic, cut_windows(): paired = jnp.where(chosen, moved, paired)  16.4 us
    slice x18, local copies, waits for them, and re-layouts, cut_windows(): paired[..., step_size:]  15.4 us
    all_to_all x1, waiting for transfers between devices, on_device(): lax.all_to_all(outgoing, 'pulse', split_axis=0, concat_axis=0, tiled=True)  11.5 us
    all_to_all x1, starting transfers between devices, on_device(): lax.all_to_all(outgoing, 'pulse', split_axis=0, concat_axis=0, tiled=True)  6.14 us
    all_to_all x1, starting transfers between devices, on_device(): lax.all_to_all(row_slots, 'pulse', split_axis=0, concat_axis=0, tiled=True)  5.91 us
    all_to_all x1, waiting for transfers between devices, on_device(): lax.all_to_all(lax.all_to_all(outgoing, 'pulse', split_axis=0, concat_axi...  5.52 us
    all_to_all x1, starting transfers between devices, on_device(): lax.all_to_all(lax.all_to_all(outgoing, 'pulse', split_axis=0, concat_axi...  3.47 us
    all_to_all x1, starting transfers between devices, on_device(): lax.all_to_all(lax.all_to_all(row_slots, 'pulse', split_axis=0, concat_ax...  3.23 us
  transfers between devices with their start and end apart: 5, of which 3 were waited for; matrix products, arithmetic and copies ran while one was open for 56% of the time, Pallas kernels for 0%

profile of v1, /device:TPU:0, one launch (start us, length us, event | category | flops | bytes accessed | tf_op | source)
XLA Modules:
  0.0 102.2 jit_solution(2727626767383465408)
XLA Ops:
  0.0 3.0 %collective-permute-start = (bf16[2,2,16384]{2,1,0:T(2,128)(2,1)}, bf16[2,2,16384]{2,1,0:T(2,128)(2,1)S(1)}, u32[]{:S(2)}, u32[]{:S(2)}) collective-permute-start(bf16[2,2,16384]{2,1,0:T(2,128)(2,1)} %param.12), channel_id=1, source_target_pairs={{0,1},{1,0},{2,3},{3,2},{4,5},{5,4},{6,7},{7,6},{8,9},{9,8},{10,11... | collective-permute-start | bytes 393224 | tf_op jit(solution)/shard_map/ppermute | solution.py:98
  6.9 5.9 %all-to-all-start = ((s32[16,2,6]{2,1,0:T(2,128)}), s32[16,2,6]{2,1,0:T(2,128)S(1)}, u32[]{:S(2)}, u32[]{:S(2)}) async-start(s32[16,2,6]{2,1,0:T(2,128)} %reshape.454), calls=%async_computation | async-start | bytes 32768 | tf_op jit(solution)/shard_map/all_to_all | solution.py:156
  22.0 42.6 %while.13 = (s32[]{:T(128)}, bf16[2,64,2,512]{3,2,1,0:T(2,128)(2,1)S(1)}, f32[2,64,2]{1,0,2:T(2,128)S(1)}, s32[2,64]{1,0:T(2,128)S(1)}, bf16[64,2,2,512]{3,2,1,0...) while((s32[]{:T(128)}, bf16[2,64,2,512]{3,2,1,0:T(2,128)(2,1)S(1)}, f32[2,64,2]{1,0,2:T(2,128)S(1)}, ...), condition=%wide.region_4.5_spmd, body=%wide.region_3.4_spmd.sunk | while | flops 3162434 | bytes 28723936 | solution.py:123
  22.3 1.1 %gather_fusion = bf16[64,2,2,512]{3,2,1,0:T(2,128)(2,1)S(1)} fusion(bf16[64,2,2,512]{3,2,1,0:T(2,128)(2,1)S(1)} %get-tuple-element.289, s32[1024]{0:T(1024)S(1)} %get-tuple-element.256), kind=kCustom, calls=%fused_computation.clone.1 | custom fusion | bytes 524544 | tf_op jit(solution)/shard_map/while/body/eval_jaxpr/gather | solution.py:49
  23.6 1.1 %gather_fusion.1 = bf16[64,2,2,512]{3,2,1,0:T(2,128)(2,1)S(1)} fusion(bf16[64,2,2,512]{3,2,1,0:T(2,128)(2,1)S(1)} %get-tuple-element.289, s32[1024]{0:T(1024)S(1)} %get-tuple-element.257), kind=kCustom, calls=%fused_computation.1.clone.1 | custom fusion | bytes 524544 | tf_op jit(solution)/shard_map/while/body/eval_jaxpr/gather | solution.py:49
  24.9 1.0 slice.134
  26.9 1.0 slice.135
  28.9 1.0 slice.136
  29.9 1.0 broadcast_select_fusion.22
  30.9 1.0 slice.137
  31.9 1.0 broadcast_select_fusion.23
  32.9 1.0 slice.138
  34.9 1.0 slice.139
  36.9 1.0 slice.140
  38.0 1.0 broadcast_select_fusion.26
  43.5 1.1 %gather_fusion = bf16[64,2,2,512]{3,2,1,0:T(2,128)(2,1)S(1)} fusion(bf16[64,2,2,512]{3,2,1,0:T(2,128)(2,1)S(1)} %get-tuple-element.289, s32[1024]{0:T(1024)S(1)} %get-tuple-element.256), kind=kCustom, calls=%fused_computation.clone.1 | custom fusion | bytes 524544 | tf_op jit(solution)/shard_map/while/body/eval_jaxpr/gather | solution.py:49
  44.8 1.1 %gather_fusion.1 = bf16[64,2,2,512]{3,2,1,0:T(2,128)(2,1)S(1)} fusion(bf16[64,2,2,512]{3,2,1,0:T(2,128)(2,1)S(1)} %get-tuple-element.289, s32[1024]{0:T(1024)S(1)} %get-tuple-element.257), kind=kCustom, calls=%fused_computation.1.clone.1 | custom fusion | bytes 524544 | tf_op jit(solution)/shard_map/while/body/eval_jaxpr/gather | solution.py:49
  46.1 1.0 slice.134
  48.2 1.0 slice.135
  50.2 1.0 slice.136
  52.2 1.0 slice.137
  54.2 1.0 slice.138
  56.2 1.0 slice.139
  58.2 1.0 slice.140
  65.0 1.0 reshape.459
  66.0 6.1 %all-to-all-start.2 = ((bf16[16,2,6,2,512]{4,3,2,1,0:T(2,128)(2,1)}), bf16[16,2,6,2,512]{4,3,2,1,0:T(2,128)(2,1)S(1)}, u32[]{:S(2)}, u32[]{:S(2)}) async-start(bf16[16,2,6,2,512]{4,3,2,1,0:T(2,128)(2,1)} %reshape.459), calls=%async_computation.2 | async-start | bytes 786432 | tf_op jit(solution)/shard_map/all_to_all | solution.py:149
  72.8 11.5 %all-to-all-done.2 = bf16[16,2,6,2,512]{4,3,2,1,0:T(2,128)(2,1)S(1)} async-done(((bf16[16,2,6,2,512]{4,3,2,1,0:T(2,128)(2,1)}), bf16[16,2,6,2,512]{4,3,2,1,0:T(2,128)(2,1)S(1)}, u32[]{:S(2)}, u32[]{:S(2)}) %all-to-all-start.2) | async-done | bytes 393248 | tf_op jit(solution)/shard_map/all_to_all | solution.py:149
  84.3 3.2 %all-to-all-start.1 = ((s32[16,2,6]{0,2,1:T(8,128)}), s32[16,2,6]{0,2,1:T(8,128)S(1)}, u32[]{:S(2)}, u32[]{:S(2)}) async-start(s32[16,2,6]{0,2,1:T(8,128)} %copy.77), calls=%async_computation.1 | async-start | bytes 16384 | tf_op jit(solution)/shard_map/all_to_all | solution.py:155
  87.5 1.0 copy.86
  88.6 2.8 %all-to-all-done.1 = s32[16,2,6]{0,2,1:T(8,128)S(1)} async-done(((s32[16,2,6]{0,2,1:T(8,128)}), s32[16,2,6]{0,2,1:T(8,128)S(1)}, u32[]{:S(2)}, u32[]{:S(2)}) %all-to-all-start.1) | async-done | bytes 800 | tf_op jit(solution)/shard_map/all_to_all | solution.py:155
  91.3 3.5 %all-to-all-start.3 = ((bf16[16,2,6,2,512]{4,3,2,0,1:T(2,128)(2,1)}), bf16[16,2,6,2,512]{4,3,2,0,1:T(2,128)(2,1)S(1)}, u32[]{:S(2)}, u32[]{:S(2)}) async-start(bf16[16,2,6,2,512]{4,3,2,0,1:T(2,128)(2,1)} %copy.86), calls=%async_computation.3 | async-start | bytes 786432 | tf_op jit(solution)/shard_map/all_to_all | solution.py:148
  95.3 5.5 %all-to-all-done.3 = bf16[16,2,6,2,512]{4,3,2,0,1:T(2,128)(2,1)S(1)} async-done(((bf16[16,2,6,2,512]{4,3,2,0,1:T(2,128)(2,1)}), bf16[16,2,6,2,512]{4,3,2,0,1:T(2,128)(2,1)S(1)}, u32[]{:S(2)}, u32[]{:S(2)}) %all-to-all-start.3) | async-done | bytes 393248 | tf_op jit(solution)/shard_map/all_to_all | solution.py:148
  (130 shorter events, 35.4 us)
Async XLA Ops:
  0.0 94.8 %copy-start = (bf16[32,2,512]{2,1,0:T(2,128)(2,1)S(1)}, bf16[32,2,512]{2,1,0:T(2,128)(2,1)}, u32[]{:S(2)}) copy-start(bf16[32,2,512]{2,1,0:T(2,128)(2,1)} %param.20) | copy-start | bytes 196612
  0.0 19.1 %collective-permute-start = (bf16[2,2,16384]{2,1,0:T(2,128)(2,1)}, bf16[2,2,16384]{2,1,0:T(2,128)(2,1)S(1)}, u32[]{:S(2)}, u32[]{:S(2)}) collective-permute-start(bf16[2,2,16384]{2,1,0:T(2,128)(2,1)} %param.12), channel_id=1, source_target_pairs={{0,1},{1,0},{2,3},{3,2},{4,5},{5,4},{6,7},{7,6},{8,9},{9,8},{10,11... | collective-permute-start | bytes 393224 | tf_op jit(solution)/shard_map/ppermute | solution.py:98
  6.9 59.1 %all-to-all-start = ((s32[16,2,6]{2,1,0:T(2,128)}), s32[16,2,6]{2,1,0:T(2,128)S(1)}, u32[]{:S(2)}, u32[]{:S(2)}) async-start(s32[16,2,6]{2,1,0:T(2,128)} %reshape.454), calls=%async_computation | async-start | bytes 32768 | tf_op jit(solution)/shard_map/all_to_all | solution.py:156
  13.6 0.7 copy-start.4
  14.7 1.5 %copy-start.5 = (f32[1,128]{1,0:T(1,128)S(1)}, f32[1,128]{1,0:T(1,128)}, u32[]{:S(2)}) copy-start(f32[1,128]{1,0:T(1,128)} %param.18) | copy-start | bytes 1540
  14.7 2.8 %copy-start.3 = (f32[1,128,2]{1,2,0:T(2,128)S(1)}, f32[1,128,2]{1,2,0:T(2,128)}, u32[]{:S(2)}) copy-start(f32[1,128,2]{1,2,0:T(2,128)} %param.14) | copy-start | bytes 3076
  14.7 3.5 %copy-start.6 = (s32[1,128]{1,0:T(1,128)S(1)}, s32[1,128]{1,0:T(1,128)}, u32[]{:S(2)}) copy-start(s32[1,128]{1,0:T(1,128)} %param.15) | copy-start | bytes 1540
  15.6 3.5 %copy-start.1 = (bf16[2,2,16384]{2,1,0:T(2,128)(2,1)S(1)}, bf16[2,2,16384]{2,1,0:T(2,128)(2,1)}, u32[]{:S(2)}) copy-start(bf16[2,2,16384]{2,1,0:T(2,128)(2,1)} %param.12) | copy-start | bytes 393220
  66.0 28.8 %copy-start.2 = (bf16[64,32]{0,1:T(8,128)(2,1)S(1)}, bf16[64,32]{0,1:T(8,128)(2,1)}, u32[]{:S(2)}) copy-start(bf16[64,32]{0,1:T(8,128)(2,1)} %param.21) | copy-start | bytes 12292
  66.0 18.3 %all-to-all-start.2 = ((bf16[16,2,6,2,512]{4,3,2,1,0:T(2,128)(2,1)}), bf16[16,2,6,2,512]{4,3,2,1,0:T(2,128)(2,1)S(1)}, u32[]{:S(2)}, u32[]{:S(2)}) async-start(bf16[16,2,6,2,512]{4,3,2,1,0:T(2,128)(2,1)} %reshape.459), calls=%async_computation.2 | async-start | bytes 786432 | tf_op jit(solution)/shard_map/all_to_all | solution.py:149
  84.3 7.0 %all-to-all-start.1 = ((s32[16,2,6]{0,2,1:T(8,128)}), s32[16,2,6]{0,2,1:T(8,128)S(1)}, u32[]{:S(2)}, u32[]{:S(2)}) async-start(s32[16,2,6]{0,2,1:T(8,128)} %copy.77), calls=%async_computation.1 | async-start | bytes 16384 | tf_op jit(solution)/shard_map/all_to_all | solution.py:155
  91.3 9.4 %all-to-all-start.3 = ((bf16[16,2,6,2,512]{4,3,2,0,1:T(2,128)(2,1)}), bf16[16,2,6,2,512]{4,3,2,0,1:T(2,128)(2,1)S(1)}, u32[]{:S(2)}, u32[]{:S(2)}) async-start(bf16[16,2,6,2,512]{4,3,2,0,1:T(2,128)(2,1)} %copy.86), calls=%async_computation.3 | async-start | bytes 786432 | tf_op jit(solution)/shard_map/all_to_all | solution.py:148
